TPU v7x, 256 devices: a whole 4x4x8 slice. The times are simulated.
256 devices in a mesh: seq: 128 (over x, y, z), head: 2 (over core).
Axes of the slice: x: 4, y: 4, z: 8, core: 2. Of those that a mesh axis runs over, the one named last changes fastest.
Arguments:
- queries: bfloat16 [32768, 4096], P('seq', 'head'), may hold values from -12 to 12
- key_states: bfloat16 [32768, 1024], P('seq', 'head'), may hold values from -12 to 12
- value_states: bfloat16 [32768, 1024], P('seq', 'head'), may hold values from -6 to 6
- positions: int32 [3, 32768], P(None, 'seq'), may hold values from 0 to 4095
- random_blocks: int32 [512, 8, 3], P('seq', 'head'), may hold values from 0 to 511, as said below
- global_blocks: int32 [2], replicated, may hold values from 0 to 511
- out_grad: bfloat16 [32768, 4096], P('seq', 'head'), may hold values from -6 to 6
Outputs:
- attended: bfloat16 [32768, 4096], P('seq', 'head')
- query_grad: bfloat16 [32768, 4096], P('seq', 'head')
- key_grad: bfloat16 [32768, 1024], P('seq', 'head')
- value_grad: bfloat16 [32768, 1024], P('seq', 'head')
Inputs may be any that keep to these rules, and one draw needn't show every extreme that they name: `random_blocks`: for each index of seq and each index of head (its 4 block rows and 4 key-value heads), at most 2 of its random blocks lie in the blocks of any one index of seq, and exactly 2 in one of them.
All inputs are finite; a program needn't handle non-finite values.
Results may differ from a plain program's by a relative error of at most 0.013.
The roundings to bfloat16 on the way count: a program that leaves them out, or rounds other values in their place, can miss the bound.
Values may be sent and summed in bfloat16 or wider, within the bound.
No kernel may reach another device: no remote copies, remote signals or barrier semaphores. Data moves between devices by JAX's collectives and lax.ppermute only.
A program may use at most 128 MiB of HBM per device.

v0:
```python
import math
import jax
import jax.numpy as jnp
from jax import lax
from jax.sharding import PartitionSpec as P

HD = 128
GROUP = 4
BLK = 64
GLOB = 2
RND = 3
NEG_FILL = -1e30
ROPE_BASE = 1000000.0


def extended(array, sides, width):
    for axis, dim in sides:
        devices, length = (lax.axis_size(axis), array.shape[dim])
        up = [(i, (i + 1) % devices) for i in range(devices - 1)]
        down = [(j, i) for i, j in up]
        last = lax.slice_in_dim(array, length - width, length, axis=dim)
        leading = lax.slice_in_dim(array, 0, width, axis=dim)
        before = lax.ppermute(last, axis, up)
        after = lax.ppermute(leading, axis, down)
        array = jnp.concatenate([before, array, after], axis=dim)
    return array


def spread(block, axis, source):
    block = jnp.where(lax.axis_index(axis) == source, block, jnp.zeros_like(block))
    return lax.psum(block, axis)


def shifted(array, axis, by):
    devices = lax.axis_size(axis)
    pairs = [(i, i + by) for i in range(devices) if 0 <= i + by < devices]
    return lax.ppermute(array, axis, pairs)


def tables(positions):
    half_dim = HD // 2
    freq_ids = jnp.arange(half_dim)
    inv_freq = jnp.power(jnp.float32(ROPE_BASE), -2.0 * freq_ids.astype(jnp.float32) / HD)
    pos_float = positions.astype(jnp.float32)
    chosen = jnp.where(
        (freq_ids % 3 == 0)[None, :],
        pos_float[0][:, None],
        jnp.where((freq_ids % 3 == 1)[None, :], pos_float[1][:, None], pos_float[2][:, None]),
    )
    angles = chosen * inv_freq[None, :]
    return (jnp.cos(angles), jnp.sin(angles))


def rotate(states, cosines, sine_vals):
    half_dim = HD // 2
    first_half = states[..., :half_dim]
    second_half = states[..., half_dim:]
    cos_b = cosines[:, None, :]
    sin_b = sine_vals[:, None, :]
    return jnp.concatenate(
        [first_half * cos_b - second_half * sin_b, second_half * cos_b + first_half * sin_b],
        axis=-1,
    )


def unrotate(states, cosines, sine_vals):
    half_dim = HD // 2
    first_half = states[..., :half_dim]
    second_half = states[..., half_dim:]
    cos_b = cosines[:, None, :]
    sin_b = sine_vals[:, None, :]
    return jnp.concatenate(
        [first_half * cos_b + second_half * sin_b, second_half * cos_b - first_half * sin_b],
        axis=-1,
    )


def attend(query_block_view, key_block_view, value_block_view, gradient_block_view, key_mask):
    score_scale = 1.0 / math.sqrt(HD)
    logit_scores = (
        jnp.einsum(
            "mtyp,mop->myto", query_block_view, key_block_view, preferred_element_type=jnp.float32
        )
        * score_scale
    )
    logit_scores = jnp.where(key_mask[:, None, None, :], logit_scores, NEG_FILL)
    row_max = jnp.max(logit_scores, axis=-1, keepdims=True)
    exponent = jnp.exp(logit_scores - row_max)
    probability = exponent / jnp.sum(exponent, axis=-1, keepdims=True)
    attention_weights = probability.astype(jnp.bfloat16)
    attended = jnp.einsum(
        "ywiu,yuz->yiwz", attention_weights, value_block_view, preferred_element_type=jnp.float32
    ).astype(jnp.bfloat16)
    weight_gradient = jnp.einsum(
        "mtyp,mop->myto", gradient_block_view, value_block_view, preferred_element_type=jnp.float32
    )
    row_delta = jnp.sum(
        gradient_block_view.astype(jnp.float32) * attended.astype(jnp.float32), axis=-1
    )
    row_delta = jnp.transpose(row_delta, (0, 2, 1))[..., None]
    score_gradient = (probability * (weight_gradient - row_delta) * score_scale).astype(
        jnp.bfloat16
    )
    value_portion = jnp.einsum(
        "pcht,phca->pta", attention_weights, gradient_block_view, preferred_element_type=jnp.float32
    )
    key_portion = jnp.einsum(
        "pcht,phca->pta", score_gradient, query_block_view, preferred_element_type=jnp.float32
    )
    query_portion = jnp.einsum(
        "ywiu,yuz->yiwz", score_gradient, key_block_view, preferred_element_type=jnp.float32
    )
    return (attended, query_portion, key_portion, value_portion)


def onehot(ids, count):
    return (ids[:, None] == jnp.arange(count, dtype=jnp.int32)[None, :]).astype(jnp.bfloat16)


def local(queries, key_states, value_states, positions, random_blocks, global_blocks, out_grad):
    tok_rows = queries.shape[0]
    block_rows = tok_rows // BLK
    kv_dev = key_states.shape[1] // HD
    seq_count = lax.axis_size("seq")
    my_index = lax.axis_index("seq")
    slot_count = block_rows * kv_dev * RND
    capacity = (slot_count + seq_count - 1) // seq_count + 1
    score_scale = 1.0 / math.sqrt(HD)
    table_rows = block_rows * kv_dev
    all_blocks = lax.all_gather(random_blocks, "seq").reshape(seq_count, slot_count)
    head_ids = jnp.broadcast_to(
        jnp.arange(kv_dev, dtype=jnp.int32)[None, :, None], (block_rows, kv_dev, RND)
    ).reshape(slot_count)
    slot_ids = jnp.arange(slot_count, dtype=jnp.int32)
    all_owners = all_blocks // block_rows
    earlier = (all_owners[:, :, None] == all_owners[:, None, :]) & (
        slot_ids[None, None, :] < slot_ids[None, :, None]
    )
    all_rank = jnp.sum(earlier, axis=2)
    all_code = all_blocks % block_rows * kv_dev + head_ids[None, :]
    mine = all_owners == my_index
    asked_part = jnp.stack(
        [jnp.sum(jnp.where(mine & (all_rank == c), all_code, 0), axis=1) for c in range(capacity)],
        axis=1,
    )
    flat_ids = random_blocks.reshape(slot_count)
    owners = flat_ids // block_rows
    my_rank = lax.dynamic_index_in_dim(all_rank, my_index, 0, keepdims=False)
    slot_pos = owners * capacity + my_rank
    cosines, sine_vals = tables(positions)
    q_rot = rotate(
        queries.reshape(tok_rows, kv_dev * GROUP, HD).astype(jnp.float32), cosines, sine_vals
    ).astype(jnp.bfloat16)
    k_rot = rotate(
        key_states.reshape(tok_rows, kv_dev, HD).astype(jnp.float32), cosines, sine_vals
    ).astype(jnp.bfloat16)
    paired = jnp.stack([k_rot.reshape(tok_rows, kv_dev * HD), value_states])
    own_blocks = paired.reshape(2, block_rows, BLK, kv_dev, HD)
    kv_table = own_blocks.transpose(1, 3, 0, 2, 4).reshape(table_rows, 2 * BLK * HD)
    asked_flat = asked_part.reshape(seq_count * capacity)
    answers = jnp.dot(
        onehot(asked_flat, table_rows), kv_table, preferred_element_type=jnp.float32
    ).astype(jnp.bfloat16)
    padded = extended(paired, (("seq", 1),), BLK)
    window_blocks = padded.reshape(2, block_rows + 2, BLK, kv_dev, HD)
    glob_owner = global_blocks // block_rows
    glob_local = global_blocks % block_rows
    glob_pieces = []
    for which_glob in range(GLOB):
        glob_piece = lax.dynamic_index_in_dim(own_blocks, glob_local[which_glob], 1, keepdims=False)
        glob_pieces.append(spread(glob_piece, "seq", glob_owner[which_glob]))
    glob_kv = jnp.stack(glob_pieces, axis=1)
    answers, padded, glob_kv = lax.optimization_barrier((answers, padded, glob_kv))
    window_blocks = padded.reshape(2, block_rows + 2, BLK, kv_dev, HD)
    fetched = lax.all_to_all(
        answers.reshape(seq_count, capacity, 2 * BLK * HD), "seq", 0, 0, tiled=True
    ).reshape(seq_count * capacity, 2 * BLK * HD)
    window_set = jnp.stack(
        [window_blocks[:, offset : offset + block_rows] for offset in range(3)], axis=2
    )
    glob_set = jnp.broadcast_to(glob_kv[:, None], (2, block_rows, GLOB, BLK, kv_dev, HD))
    near_set = jnp.concatenate([window_set, glob_set], axis=2).reshape(
        2, block_rows, (3 + GLOB) * BLK, kv_dev, HD
    )
    window_ids = (
        my_index * block_rows + jnp.arange(block_rows)[:, None] + jnp.arange(-1, 2)[None, :]
    )
    window_ok = (window_ids >= 0) & (window_ids < seq_count * block_rows)
    near_ok = jnp.concatenate([window_ok, jnp.ones((block_rows, GLOB), dtype=bool)], axis=1)
    near_mask = jnp.repeat(near_ok, BLK, axis=1)
    query_nat = q_rot.reshape(block_rows, BLK, kv_dev, GROUP, HD)
    grad_nat = out_grad.reshape(block_rows, BLK, kv_dev, GROUP, HD)
    near_k = near_set[0]
    near_v = near_set[1]
    near_scores = (
        jnp.einsum("rthgd,rkhd->rhgtk", query_nat, near_k, preferred_element_type=jnp.float32)
        * score_scale
    )
    near_scores = jnp.where(near_mask[:, None, None, None, :], near_scores, NEG_FILL)
    near_wgrad = jnp.einsum(
        "rthgd,rkhd->rhgtk", grad_nat, near_v, preferred_element_type=jnp.float32
    )
    random_kv = fetched[slot_pos].reshape(block_rows, kv_dev, RND, 2, BLK, HD)
    far_k = random_kv[:, :, :, 0].reshape(block_rows, kv_dev, RND * BLK, HD)
    far_v = random_kv[:, :, :, 1].reshape(block_rows, kv_dev, RND * BLK, HD)
    far_scores = (
        jnp.einsum("rthgd,rhkd->rhgtk", query_nat, far_k, preferred_element_type=jnp.float32)
        * score_scale
    )
    far_wgrad = jnp.einsum("rthgd,rhkd->rhgtk", grad_nat, far_v, preferred_element_type=jnp.float32)
    row_max = jnp.maximum(
        jnp.max(near_scores, axis=-1, keepdims=True), jnp.max(far_scores, axis=-1, keepdims=True)
    )
    near_exp = jnp.exp(near_scores - row_max)
    far_exp = jnp.exp(far_scores - row_max)
    total = jnp.sum(near_exp, axis=-1, keepdims=True) + jnp.sum(far_exp, axis=-1, keepdims=True)
    near_prob = near_exp / total
    far_prob = far_exp / total
    near_w = near_prob.astype(jnp.bfloat16)
    far_w = far_prob.astype(jnp.bfloat16)
    attended = (
        jnp.einsum("rhgtk,rkhd->rthgd", near_w, near_v, preferred_element_type=jnp.float32)
        + jnp.einsum("rhgtk,rhkd->rthgd", far_w, far_v, preferred_element_type=jnp.float32)
    ).astype(jnp.bfloat16)
    row_delta = jnp.sum(grad_nat.astype(jnp.float32) * attended.astype(jnp.float32), axis=-1)
    row_delta = row_delta.transpose(0, 2, 3, 1)[..., None]
    near_sgrad = (near_prob * (near_wgrad - row_delta) * score_scale).astype(jnp.bfloat16)
    far_sgrad = (far_prob * (far_wgrad - row_delta) * score_scale).astype(jnp.bfloat16)
    far_kgrad = jnp.einsum(
        "rhgtk,rthgd->rhkd", far_sgrad, query_nat, preferred_element_type=jnp.float32
    )
    far_vgrad = jnp.einsum("rhgtk,rthgd->rhkd", far_w, grad_nat, preferred_element_type=jnp.float32)
    random_grad = (
        jnp.stack(
            [
                far_kgrad.reshape(block_rows, kv_dev, RND, BLK, HD),
                far_vgrad.reshape(block_rows, kv_dev, RND, BLK, HD),
            ],
            axis=3,
        )
        .reshape(slot_count, 2 * BLK * HD)
        .astype(jnp.bfloat16)
    )
    outgoing = jnp.dot(
        onehot(slot_pos, seq_count * capacity).T, random_grad, preferred_element_type=jnp.float32
    ).astype(jnp.bfloat16)
    query_portion = jnp.einsum(
        "rhgtk,rkhd->rthgd", near_sgrad, near_k, preferred_element_type=jnp.float32
    ) + jnp.einsum("rhgtk,rhkd->rthgd", far_sgrad, far_k, preferred_element_type=jnp.float32)
    near_kgrad = jnp.einsum(
        "rhgtk,rthgd->rkhd", near_sgrad, query_nat, preferred_element_type=jnp.float32
    )
    near_vgrad = jnp.einsum(
        "rhgtk,rthgd->rkhd", near_w, grad_nat, preferred_element_type=jnp.float32
    )
    near_grad = jnp.stack([near_kgrad, near_vgrad]).reshape(
        2, block_rows, 3 + GLOB, BLK, kv_dev, HD
    )
    window_acc = jnp.pad(near_grad[:, :, 0], ((0, 0), (0, 2), (0, 0), (0, 0), (0, 0)))
    window_acc = window_acc + jnp.pad(near_grad[:, :, 1], ((0, 0), (1, 1), (0, 0), (0, 0), (0, 0)))
    window_acc = window_acc + jnp.pad(near_grad[:, :, 2], ((0, 0), (2, 0), (0, 0), (0, 0), (0, 0)))
    glob_local_grad = jnp.sum(near_grad[:, :, 3:], axis=1)
    from_right = shifted(window_acc[:, 0].astype(jnp.bfloat16), "seq", -1).astype(jnp.float32)
    from_left = shifted(window_acc[:, block_rows + 1].astype(jnp.bfloat16), "seq", 1).astype(
        jnp.float32
    )
    glob_grad = lax.psum(glob_local_grad, "seq")
    outgoing, from_right, from_left, glob_grad = lax.optimization_barrier(
        (outgoing, from_right, from_left, glob_grad)
    )
    returned = lax.all_to_all(
        outgoing.reshape(seq_count, capacity, 2 * BLK * HD), "seq", 0, 0, tiled=True
    ).reshape(seq_count * capacity, 2 * BLK * HD)
    kv_grad = window_acc[:, 1 : block_rows + 1]
    kv_grad = kv_grad.at[:, block_rows - 1].add(from_right).at[:, 0].add(from_left)
    glob_mine = jnp.where((glob_owner == my_index)[None, :, None, None, None], glob_grad, 0.0)
    kv_grad = kv_grad.at[:, glob_local].add(glob_mine)
    collected = jnp.dot(
        onehot(asked_flat, table_rows).T, returned, preferred_element_type=jnp.float32
    ).reshape(block_rows, kv_dev, 2, BLK, HD)
    kv_grad = kv_grad + collected.transpose(2, 0, 3, 1, 4)
    attended = attended.reshape(tok_rows, kv_dev * GROUP * HD)
    query_grad = (
        unrotate(query_portion.reshape(tok_rows, kv_dev * GROUP, HD), cosines, sine_vals)
        .astype(jnp.bfloat16)
        .reshape(tok_rows, kv_dev * GROUP * HD)
    )
    key_acc = kv_grad[0].reshape(tok_rows, kv_dev, HD)
    key_grad = (
        unrotate(key_acc, cosines, sine_vals).astype(jnp.bfloat16).reshape(tok_rows, kv_dev * HD)
    )
    value_grad = kv_grad[1].reshape(tok_rows, kv_dev * HD).astype(jnp.bfloat16)
    return (attended, query_grad, key_grad, value_grad)


def solution(mesh):
    in_specs = (
        P("seq", "head"),
        P("seq", "head"),
        P("seq", "head"),
        P(None, "seq"),
        P("seq", "head", None),
        P(),
        P("seq", "head"),
    )
    out_specs = (P("seq", "head"), P("seq", "head"), P("seq", "head"), P("seq", "head"))
    return jax.shard_map(local, mesh=mesh, in_specs=in_specs, out_specs=out_specs, check_vma=False)
```

profile of v0, /device:TPU:32, one launch (start us, length us, event | category | flops | bytes accessed | tf_op | source)
XLA Modules:
  0.0 1072.5 jit_solution(8341888297970544012)
XLA Ops:
  11.5 3.8 collective-permute-start
  15.4 2.7 collective-permute-start.1
  27.1 348.5 %all-gather = s32[512,4,3]{2,1,0:T(4,128)S(1)} all-gather(s32[4,4,3]{2,1,0:T(4,128)S(1)} %copy.280), channel_id=2, replica_groups=mesh['seq'=128,'head'=2] {'seq'}, dimensions={0}, use_global_device_ids=true | all-gather | bytes 24768 | tf_op jit(solution)/shard_map/all_gather | solution.py:130
  378.6 3.4 copy.336
  383.5 5.7 convolution_convert_fusion.1
  389.2 2.4 pad_maximum_fusion.4
  392.5 14.2 %reshape.604 = bf16[128,2,16384]{2,1,0:T(2,128)(2,1)} reshape(bf16[256,16384]{1,0:T(8,128)(2,1)} %convolution_convert_fusion.1) | data formatting | bytes 16777216 | tf_op jit(solution)/shard_map/reshape | solution.py:176
  406.7 14.0 %all-to-all-start = ((bf16[128,2,16384]{2,1,0:T(2,128)(2,1)}), bf16[128,2,16384]{2,1,0:T(2,128)(2,1)}, u32[]{:S(2)}, u32[]{:S(2)}) async-start(bf16[128,2,16384]{2,1,0:T(2,128)(2,1)} %reshape.604), calls=%async_computation | async-start | bytes 16777216 | tf_op jit(solution)/shard_map/all_to_all | solution.py:175
  421.9 1.5 reshape.609
  429.2 1.4 copy.294
  432.5 1.7 fusion.54
  435.3 3.7 bitcast_reduce_fusion
  439.0 112.6 %all-to-all-done = bf16[128,2,16384]{2,1,0:T(2,128)(2,1)} async-done(((bf16[128,2,16384]{2,1,0:T(2,128)(2,1)}), bf16[128,2,16384]{2,1,0:T(2,128)(2,1)}, u32[]{:S(2)}, u32[]{:S(2)}) %all-to-all-start) | async-done | bytes 8388640 | tf_op jit(solution)/shard_map/all_to_all | solution.py:175
  551.5 13.1 %reshape.605 = bf16[256,16384]{1,0:T(8,128)(2,1)} reshape(bf16[128,2,16384]{2,1,0:T(2,128)(2,1)} %all-to-all-done) | data formatting | bytes 16777216 | tf_op jit(solution)/shard_map/reshape | solution.py:177
  564.7 7.4 gather_fusion
  573.5 1.5 fusion.11
  575.6 1.9 fusion.5
  577.6 3.6 bitcast_convert_fusion
  581.2 2.1 fusion.14
  583.3 3.0 multiply_reduce_fusion
  586.3 2.1 fusion.8
  588.4 2.8 fusion.2
  591.3 4.0 fusion.12
  596.3 2.0 copy_dynamic-update-slice_fusion.1
  598.3 2.1 copy_dynamic-update-slice_fusion
  600.4 2.3 copy-done.2
  603.9 2.1 slice_bitcast_fusion.2
  606.0 1.8 bitcast_convert_fusion.1
  607.8 1.8 fusion.53
  610.3 1.3 pad_maximum_fusion.1
  612.3 1.9 collective-permute-start.3
  614.3 3.9 collective-permute-start.2
  618.2 5.7 convolution_convert_fusion
  624.7 197.6 %all-reduce.8.cloned.1.call-done = f32[2,2,64,4,128]{4,3,2,0,1:T(4,128)} async-done(((f32[2,2,64,4,128]{4,3,2,0,1:T(4,128)}), f32[2,2,64,4,128]{4,3,2,0,1:T(4,128)}) %all-reduce.8.cloned.1.call-update) | async-done | bytes 524304 | tf_op jit(solution)/shard_map/psum | solution.py:267
  822.3 14.2 %reshape.614 = bf16[128,2,16384]{2,1,0:T(2,128)(2,1)} reshape(bf16[256,16384]{1,0:T(8,128)(2,1)} %convolution_convert_fusion) | data formatting | bytes 16777216 | tf_op jit(solution)/shard_map/reshape | solution.py:272
  836.5 11.2 %all-to-all-start.1 = ((bf16[128,2,16384]{2,1,0:T(2,128)(2,1)}), bf16[128,2,16384]{2,1,0:T(2,128)(2,1)}, u32[]{:S(2)}, u32[]{:S(2)}) async-start(bf16[128,2,16384]{2,1,0:T(2,128)(2,1)} %reshape.614), calls=%async_computation.1 | async-start | bytes 16777216 | tf_op jit(solution)/shard_map/all_to_all | solution.py:271
  847.7 3.2 copy.304
  851.0 2.6 reshape.608
  853.6 2.4 fusion.61
  857.0 2.1 fusion.55
  859.1 2.2 copy.340
  861.2 1.6 copy.339
  862.8 1.6 add_convert_fusion.1
  864.5 1.4 copy.325
  867.5 163.5 %all-to-all-done.1 = bf16[128,2,16384]{2,1,0:T(2,128)(2,1)} async-done(((bf16[128,2,16384]{2,1,0:T(2,128)(2,1)}), bf16[128,2,16384]{2,1,0:T(2,128)(2,1)}, u32[]{:S(2)}, u32[]{:S(2)}) %all-to-all-start.1) | async-done | bytes 8388640 | tf_op jit(solution)/shard_map/all_to_all | solution.py:271
  1031.0 13.1 %reshape.615 = bf16[256,16384]{1,0:T(8,128)(2,1)} reshape(bf16[128,2,16384]{2,1,0:T(2,128)(2,1)} %all-to-all-done.1) | data formatting | bytes 16777216 | tf_op jit(solution)/shard_map/reshape | solution.py:273
  1044.2 12.0 %copy.318 = bf16[256,16384]{0,1:T(8,128)(2,1)} copy(bf16[256,16384]{1,0:T(8,128)(2,1)} %reshape.615) | data formatting | bytes 16777216 | tf_op jit(solution)/shard_map/reshape | solution.py:273
  1056.2 5.7 fusion.17
  (153 shorter events, 35.7 us)
Async XLA Ops:
  7.2 14.8 %copy-start.15 = (bf16[256,512]{1,0:T(8,128)(2,1)S(1)}, bf16[256,512]{1,0:T(8,128)(2,1)}, u32[]{:S(2)}) copy-start(bf16[256,512]{1,0:T(8,128)(2,1)} %param.13) | copy-start | bytes 786436
  7.2 10.9 %copy-start.20 = (s32[2]{0:T(128)S(1)}, s32[2]{0:T(128)}, u32[]{:S(2)}) copy-start(s32[2]{0:T(128)} %param.16) | copy-start | bytes 28
  7.2 384.4 %all-reduce.10.cloned.1.call-start = ((), (), s32[]{:S(2)}) async-start(), calls=%async_computation.3 | async-start | bytes 524288 | tf_op jit(solution)/shard_map/psum | solution.py:31
  10.5 16.2 %copy-start.17 = (s32[4,4,3]{1,0,2:T(4,128)S(1)}, s32[4,4,3]{1,0,2:T(4,128)}, u32[]{:S(2)}) copy-start(s32[4,4,3]{1,0,2:T(4,128)} %param.15) | copy-start | bytes 580
  11.5 377.6 %collective-permute-start = (bf16[2,64,512]{1,2,0:T(8,128)(2,1)}, bf16[2,64,512]{1,2,0:T(8,128)(2,1)}, u32[]{:S(2)}, u32[]{:S(2)}) collective-permute-start(bf16[2,64,512]{1,2,0:T(8,128)(2,1)} %get-tuple-element.102), channel_id=1, source_target_pairs={{0,2},{2,4},{4,6},{6,8},{8,10},{10,12},{12,14},{14,16},{16,18},{18... | collective-permute-start | bytes 393224 | tf_op jit(solution)/shard_map/ppermute | solution.py:23
  15.4 373.8 %collective-permute-start.1 = (bf16[2,64,512]{1,2,0:T(8,128)(2,1)}, bf16[2,64,512]{1,2,0:T(8,128)(2,1)}, u32[]{:S(2)}, u32[]{:S(2)}) collective-permute-start(bf16[2,64,512]{1,2,0:T(8,128)(2,1)} %get-tuple-element.103), channel_id=1, source_target_pairs={{2,0},{4,2},{6,4},{8,6},{10,8},{12,10},{14,12},{16,14},{18,16},{20... | collective-permute-start | bytes 393224 | tf_op jit(solution)/shard_map/ppermute | solution.py:24
  377.2 0.6 copy-start.16
  406.7 15.2 %copy-start.12 = (bf16[256,2048]{1,0:T(8,128)(2,1)S(1)}, bf16[256,2048]{1,0:T(8,128)(2,1)}, u32[]{:S(2)}) copy-start(bf16[256,2048]{1,0:T(8,128)(2,1)} %param.17) | copy-start | bytes 3145732
  406.7 16.7 %copy-start.13 = (bf16[256,2048]{1,0:T(8,128)(2,1)S(1)}, bf16[256,2048]{1,0:T(8,128)(2,1)}, u32[]{:S(2)}) copy-start(bf16[256,2048]{1,0:T(8,128)(2,1)} %param.11) | copy-start | bytes 3145732
  406.7 144.8 %all-to-all-start = ((bf16[128,2,16384]{2,1,0:T(2,128)(2,1)}), bf16[128,2,16384]{2,1,0:T(2,128)(2,1)}, u32[]{:S(2)}, u32[]{:S(2)}) async-start(bf16[128,2,16384]{2,1,0:T(2,128)(2,1)} %reshape.604), calls=%async_computation | async-start | bytes 16777216 | tf_op jit(solution)/shard_map/all_to_all | solution.py:175
  420.7 401.6 %all-reduce.8.cloned.1.call-start = ((), (), s32[]{:S(2)}) async-start(), calls=%async_computation.2 | async-start | bytes 1048576 | tf_op jit(solution)/shard_map/psum | solution.py:267
  434.2 1.1 copy-start.3
  572.4 2.5 slice-start
  572.6 2.4 copy-start.6
  572.6 3.0 slice-start.1
  575.6 2.0 copy-start.14
  577.6 3.6 copy-start.10
  588.4 17.6 %copy-start.4 = (bf16[4,4,4,64,192]{4,3,2,1,0:T(8,128)(2,1)}, bf16[4,4,4,64,192]{4,3,2,1,0:T(8,128)(2,1)S(1)}, u32[]{:S(2)}) copy-start(bf16[4,4,4,64,192]{4,3,2,1,0:T(8,128)(2,1)S(1)} %fusion.8) | copy-start | bytes 4718596
  591.3 4.0 copy-start
  600.4 2.3 copy-start.2
  607.8 2.5 copy-start.9
  612.3 11.6 %collective-permute-start.3 = (bf16[2,64,4,128]{3,2,1,0:T(4,128)(2,1)S(1)}, bf16[2,64,4,128]{3,2,1,0:T(4,128)(2,1)S(1)}, u32[]{:S(2)}, u32[]{:S(2)}) collective-permute-start(bf16[2,64,4,128]{3,2,1,0:T(4,128)(2,1)S(1)} %get-tuple-element.89), channel_id=1, source_target_pairs={{0,2},{2,4},{4,6},{6,8},{8,10},{10,12},{12,14},{14,16},{16,18},{18... | collective-permute-start | bytes 393224 | tf_op jit(solution)/shard_map/ppermute | solution.py:37
  614.3 9.7 collective-permute-start.2
  836.5 194.6 %all-to-all-start.1 = ((bf16[128,2,16384]{2,1,0:T(2,128)(2,1)}), bf16[128,2,16384]{2,1,0:T(2,128)(2,1)}, u32[]{:S(2)}, u32[]{:S(2)}) async-start(bf16[128,2,16384]{2,1,0:T(2,128)(2,1)} %reshape.614), calls=%async_computation.1 | async-start | bytes 16777216 | tf_op jit(solution)/shard_map/all_to_all | solution.py:271
  847.7 5.9 copy-start.1
  853.6 2.4 copy-start.5
  853.6 2.4 copy-start.7
  862.8 3.2 copy-start.8
  864.4 1.6 copy-start.18
  866.0 1.4 copy-start.11
  1056.2 5.8 copy-start.19
Sparse Core Ops, SparseCore 0:
  26.8 218.4 all-reduce.9
  610.4 211.8 all-reduce.7
where the time goes:
time: 1080 us; the launch traced here: 1070 us
  waiting for transfers between devices  474 us (44%)
  blocking collectives  348 us (32%)
  local copies, waits for them, and re-layouts  123 us (11%)
  matrix products  45.1 us (4%)
  starting transfers between devices  37.8 us (3%)
  other arithmetic  23.6 us (2%)
  between operations  20.4 us (2%)
    all_gather x1, blocking collectives, local(): lax.all_gather(random_blocks, 'seq').reshape(seq_count, slot_count)  348 us
    psum x1, waiting for transfers between devices, local(): glob_grad = lax.psum(glob_local_grad, 'seq')  198 us
    all_to_all x1, waiting for transfers between devices, local(): lax.all_to_all(outgoing.reshape(seq_count, capacity, 2 * BLK * HD), 'seq'...  164 us
    all_to_all x1, waiting for transfers between devices, local(): lax.all_to_all(answers.reshape(seq_count, capacity, 2 * BLK * HD), 'seq',...  113 us
    reshape x2, local copies, waits for them, and re-layouts, local(): returned = lax.all_to_all(outgoing.reshape(seq_count, capacity, 2 * BLK *...  25.1 us
  transfers between devices with their start and end apart: 8, of which 3 were waited for; matrix products, arithmetic and copies ran while one was open for 6% of the time, Pallas kernels for 0%

commit v1 on v0

--- a/solution.py
+++ b/solution.py
@@ -264,7 +264,7 @@
     from_left = shifted(window_acc[:, block_rows + 1].astype(jnp.bfloat16), "seq", 1).astype(
         jnp.float32
     )
-    glob_grad = lax.psum(glob_local_grad, "seq")
+    glob_grad = jnp.sum(lax.all_gather(glob_local_grad, "seq"), axis=0)
     outgoing, from_right, from_left, glob_grad = lax.optimization_barrier(
         (outgoing, from_right, from_left, glob_grad)
     )

time: 1080 us -> 1220 us (1.13)
  waiting for transfers between devices: 474 us -> 584 us
  other arithmetic: 23.6 us -> 44.3 us
    all_gather x0 -> x1, waiting for transfers between devices: none -> 305 us  [local(): glob_grad = jnp.sum(lax.all_gather(glob_local_grad, 'seq'), axis=0)]
    psum x1 -> x0, waiting for transfers between devices: 198 us -> none  [local(): glob_grad = lax.psum(glob_local_grad, 'seq')]
    reduce_sum x0 -> x1, other arithmetic: none -> 21.7 us  [local(): glob_grad = jnp.sum(lax.all_gather(glob_local_grad, 'seq'), axis=0)]
where the time goes in v1:
time: 1220 us; the launch traced here: 1210 us
  waiting for transfers between devices  584 us (48%)
  blocking collectives  348 us (29%)
  local copies, waits for them, and re-layouts  128 us (10%)
  matrix products  45.4 us (4%)
  other arithmetic  44.3 us (4%)
  starting transfers between devices  38.3 us (3%)
  between operations  20.3 us (2%)
    all_gather x1, blocking collectives, local(): lax.all_gather(random_blocks, 'seq').reshape(seq_count, slot_count)  348 us
    all_gather x1, waiting for transfers between devices, local(): glob_grad = jnp.sum(lax.all_gather(glob_local_grad, 'seq'), axis=0)  305 us
    all_to_all x1, waiting for transfers between devices, local(): lax.all_to_all(outgoing.reshape(seq_count, capacity, 2 * BLK * HD), 'seq'...  166 us
    all_to_all x1, waiting for transfers between devices, local(): lax.all_to_all(answers.reshape(seq_count, capacity, 2 * BLK * HD), 'seq',...  114 us
    reshape x2, local copies, waits for them, and re-layouts, local(): returned = lax.all_to_all(outgoing.reshape(seq_count, capacity, 2 * BLK *...  25 us
  transfers between devices with their start and end apart: 8, of which 3 were waited for; matrix products, arithmetic and copies ran while one was open for 6% of the time, Pallas kernels for 0%

profile of v1, /device:TPU:32, one launch (start us, length us, event | category | flops | bytes accessed | tf_op | source)
XLA Modules:
  0.0 1208.7 jit_solution(12723237033564684314)
XLA Ops:
  11.5 3.8 collective-permute-start
  15.4 2.7 collective-permute-start.1
  27.1 348.3 %all-gather = s32[512,4,3]{2,1,0:T(4,128)S(1)} all-gather(s32[4,4,3]{2,1,0:T(4,128)S(1)} %copy.327), channel_id=2, replica_groups=mesh['seq'=128,'head'=2] {'seq'}, dimensions={0}, use_global_device_ids=true | all-gather | bytes 24768 | tf_op jit(solution)/shard_map/all_gather | solution.py:130
  378.4 3.4 copy.384
  383.3 5.6 convolution_convert_fusion.1
  389.0 2.4 pad_maximum_fusion.4
  392.3 14.2 %reshape.604 = bf16[128,2,16384]{2,1,0:T(2,128)(2,1)} reshape(bf16[256,16384]{1,0:T(8,128)(2,1)} %convolution_convert_fusion.1) | data formatting | bytes 16777216 | tf_op jit(solution)/shard_map/reshape | solution.py:176
  406.5 14.0 %all-to-all-start = ((bf16[128,2,16384]{2,1,0:T(2,128)(2,1)}), bf16[128,2,16384]{2,1,0:T(2,128)(2,1)}, u32[]{:S(2)}, u32[]{:S(2)}) async-start(bf16[128,2,16384]{2,1,0:T(2,128)(2,1)} %reshape.604), calls=%async_computation | async-start | bytes 16777216 | tf_op jit(solution)/shard_map/all_to_all | solution.py:175
  421.1 1.5 reshape.609
  428.2 1.4 copy.341
  431.5 1.6 fusion.54
  434.1 3.7 bitcast_reduce_fusion
  437.8 113.6 %all-to-all-done = bf16[128,2,16384]{2,1,0:T(2,128)(2,1)} async-done(((bf16[128,2,16384]{2,1,0:T(2,128)(2,1)}), bf16[128,2,16384]{2,1,0:T(2,128)(2,1)}, u32[]{:S(2)}, u32[]{:S(2)}) %all-to-all-start) | async-done | bytes 8388640 | tf_op jit(solution)/shard_map/all_to_all | solution.py:175
  551.4 13.1 %reshape.605 = bf16[256,16384]{1,0:T(8,128)(2,1)} reshape(bf16[128,2,16384]{2,1,0:T(2,128)(2,1)} %all-to-all-done) | data formatting | bytes 16777216 | tf_op jit(solution)/shard_map/reshape | solution.py:177
  564.5 7.4 gather_fusion
  573.3 1.5 fusion.11
  576.9 2.4 fusion.5
  579.3 2.1 fusion.14
  581.5 3.6 fusion.12
  585.1 2.9 multiply_reduce_fusion
  588.0 2.8 fusion.2
  592.5 1.9 copy_dynamic-update-slice_fusion.1
  594.5 2.1 copy_dynamic-update-slice_fusion
  596.6 2.4 copy-done.4
  600.3 4.3 fusion.8
  606.8 2.9 bitcast_convert_fusion
  610.8 2.2 slice_bitcast_fusion.2
  613.0 1.7 fusion.53
  614.8 2.1 collective-permute-start.3
  616.9 3.7 collective-permute-start.2
  620.7 5.7 convolution_convert_fusion
  627.1 304.9 %all-gather.4.cloned.1.call-done = f32[256,2,64,4,128]{4,2,3,1,0:T(8,128)} async-done(((f32[2,2,64,4,128]{4,2,3,1,0:T(8,128)}), f32[256,2,64,4,128]{4,2,3,1,0:T(8,128)}) %all-gather.4.cloned.1.call-update) | async-done | bytes 67108880 | tf_op jit(solution)/shard_map/all_gather | solution.py:267
  932.0 21.7 %reduce_sum.79 = f32[2,2,64,4,128]{4,2,3,1,0:T(8,128)} reduce(f32[128,2,2,64,4,128]{5,3,4,2,1,0:T(8,128)} %bitcast.72, f32[]{:T(128)} %constant.174.clone.1), dimensions={0}, to_apply=%region_11.12 | reduce | flops 16646144 | bytes 67633152 | tf_op jit(solution)/shard_map/reduce_sum | solution.py:267
  953.7 14.1 %reshape.614 = bf16[128,2,16384]{2,1,0:T(2,128)(2,1)} reshape(bf16[256,16384]{1,0:T(8,128)(2,1)} %convolution_convert_fusion) | data formatting | bytes 16777216 | tf_op jit(solution)/shard_map/reshape | solution.py:272
  967.8 11.7 all-to-all-start.1
  979.6 3.2 copy.351
  982.7 2.6 reshape.608
  985.4 2.4 fusion.61
  988.8 2.1 fusion.55
  990.8 2.2 copy.388
  993.0 1.6 copy.387
  994.6 1.6 add_convert_fusion.1
  996.3 1.4 copy.373
  999.8 1.7 fusion.31
  1001.5 165.6 %all-to-all-done.1 = bf16[128,2,16384]{2,1,0:T(2,128)(2,1)} async-done(((bf16[128,2,16384]{2,1,0:T(2,128)(2,1)}), bf16[128,2,16384]{2,1,0:T(2,128)(2,1)}, u32[]{:S(2)}, u32[]{:S(2)}) %all-to-all-start.1) | async-done | bytes 8388640 | tf_op jit(solution)/shard_map/all_to_all | solution.py:271
  1167.1 13.1 %reshape.615 = bf16[256,16384]{1,0:T(8,128)(2,1)} reshape(bf16[128,2,16384]{2,1,0:T(2,128)(2,1)} %all-to-all-done.1) | data formatting | bytes 16777216 | tf_op jit(solution)/shard_map/reshape | solution.py:273
  1180.2 12.0 copy.366
  1192.2 5.9 fusion.17
  (169 shorter events, 39.6 us)
Async XLA Ops:
  7.2 14.8 %copy-start.18 = (bf16[256,512]{1,0:T(8,128)(2,1)S(1)}, bf16[256,512]{1,0:T(8,128)(2,1)}, u32[]{:S(2)}) copy-start(bf16[256,512]{1,0:T(8,128)(2,1)} %param.13) | copy-start | bytes 786436
  7.2 10.9 copy-start.27
  7.2 384.2 %all-reduce.7.cloned.1.call-start = ((), (), s32[]{:S(2)}) async-start(), calls=%async_computation.3 | async-start | bytes 524288 | tf_op jit(solution)/shard_map/psum | solution.py:31
  10.5 16.2 %copy-start.22 = (s32[4,4,3]{1,0,2:T(4,128)S(1)}, s32[4,4,3]{1,0,2:T(4,128)}, u32[]{:S(2)}) copy-start(s32[4,4,3]{1,0,2:T(4,128)} %param.15) | copy-start | bytes 580
  11.5 377.4 %collective-permute-start = (bf16[2,64,512]{1,2,0:T(8,128)(2,1)}, bf16[2,64,512]{1,2,0:T(8,128)(2,1)}, u32[]{:S(2)}, u32[]{:S(2)}) collective-permute-start(bf16[2,64,512]{1,2,0:T(8,128)(2,1)} %get-tuple-element.106), channel_id=1, source_target_pairs={{0,2},{2,4},{4,6},{6,8},{8,10},{10,12},{12,14},{14,16},{16,18},{18... | collective-permute-start | bytes 393224 | tf_op jit(solution)/shard_map/ppermute | solution.py:23
  15.4 373.6 %collective-permute-start.1 = (bf16[2,64,512]{1,2,0:T(8,128)(2,1)}, bf16[2,64,512]{1,2,0:T(8,128)(2,1)}, u32[]{:S(2)}, u32[]{:S(2)}) collective-permute-start(bf16[2,64,512]{1,2,0:T(8,128)(2,1)} %get-tuple-element.107), channel_id=1, source_target_pairs={{2,0},{4,2},{6,4},{8,6},{10,8},{12,10},{14,12},{16,14},{18,16},{20... | collective-permute-start | bytes 393224 | tf_op jit(solution)/shard_map/ppermute | solution.py:24
  377.0 0.6 copy-start.19
  383.3 5.7 copy-start.20
  406.5 14.6 %copy-start.14 = (bf16[256,2048]{1,0:T(8,128)(2,1)S(1)}, bf16[256,2048]{1,0:T(8,128)(2,1)}, u32[]{:S(2)}) copy-start(bf16[256,2048]{1,0:T(8,128)(2,1)} %param.17) | copy-start | bytes 3145732
  406.5 16.1 %copy-start.15 = (bf16[256,2048]{1,0:T(8,128)(2,1)S(1)}, bf16[256,2048]{1,0:T(8,128)(2,1)}, u32[]{:S(2)}) copy-start(bf16[256,2048]{1,0:T(8,128)(2,1)} %param.11) | copy-start | bytes 3145732
  406.5 144.9 %all-to-all-start = ((bf16[128,2,16384]{2,1,0:T(2,128)(2,1)}), bf16[128,2,16384]{2,1,0:T(2,128)(2,1)}, u32[]{:S(2)}, u32[]{:S(2)}) async-start(bf16[128,2,16384]{2,1,0:T(2,128)(2,1)} %reshape.604), calls=%async_computation | async-start | bytes 16777216 | tf_op jit(solution)/shard_map/all_to_all | solution.py:175
  420.5 511.5 %all-gather.4.cloned.1.call-start = ((), (), s32[]{:S(2)}) async-start(), calls=%async_computation.2 | async-start | bytes 67633152 | tf_op jit(solution)/shard_map/all_gather | solution.py:267
  427.1 0.5 copy-start.25
  433.1 1.1 copy-start.5
  572.3 3.8 slice-start
  572.4 2.4 copy-start.8
  572.4 4.5 slice-start.1
  573.3 11.8 copy-start
  576.9 2.4 copy-start.12
  579.3 2.2 copy-start.16
  590.8 1.7 copy-start.2
  596.6 2.4 copy-start.4
  599.0 1.3 copy-start.26
  599.0 1.3 copy-start.17
  600.3 6.5 copy-start.1
  604.6 1.4 copy-start.6
  614.8 11.6 collective-permute-start.3
  616.9 9.5 collective-permute-start.2
  967.8 199.3 %all-to-all-start.1 = ((bf16[128,2,16384]{2,1,0:T(2,128)(2,1)}), bf16[128,2,16384]{2,1,0:T(2,128)(2,1)}, u32[]{:S(2)}, u32[]{:S(2)}) async-start(bf16[128,2,16384]{2,1,0:T(2,128)(2,1)} %reshape.614), calls=%async_computation.1 | async-start | bytes 16777216 | tf_op jit(solution)/shard_map/all_to_all | solution.py:271
  979.6 5.8 copy-start.3
  985.4 2.4 copy-start.7
  985.4 2.4 copy-start.9
  994.6 3.2 copy-start.10
  996.2 2.6 copy-start.11
  996.2 2.6 copy-start.23
  997.7 1.2 copy-start.13
  1180.2 12.0 copy-start.21
  1192.2 6.1 copy-start.24
Sparse Core Ops, SparseCore 0:
  26.7 218.4 all-reduce.6
  600.3 331.6 all-gather.3
